TPU v7x, 512 devices: a whole 4x8x8 slice. The times are simulated.
512 devices in a mesh: fsdp: 128 (over z, x_lo, y), dp: 4 (over x_hi, core).
Axes of the slice: x: 4 (x_hi: 2, x_lo: 2; x = x_hi * 2 + x_lo), y: 8, z: 8, core: 2. Of those that a mesh axis runs over, the one named last changes fastest.
Arguments:
- glu_input: bfloat16 [131072, 3072], P(('fsdp', 'dp')), may hold values from -6 to 6
- frame_counts: int32 [512, 8], P(('fsdp', 'dp')), may hold values from 1 to 128, as said below
- send_rows: int32 [512, 256], P(('fsdp', 'dp')), may hold values from 0 to 256, as said below
- owner_rows: int32 [512, 160], P(('fsdp', 'dp')), may hold values from 0 to 255, as said below
- depth_kernel: float32 [5, 1536], replicated, may hold values from -2.5 to 2.5
- norm_gain: float32 [1536], replicated, may hold values from 0.25 to 1.75
- norm_bias: float32 [1536], replicated, may hold values from -3 to 3
- point_weight: bfloat16 [1536, 1536], P('fsdp'), may hold values from -0.15625 to 0.15625
- cotangent: bfloat16 [81920, 1536], P(('fsdp', 'dp')), may hold values from -6 to 6
Outputs:
- output: bfloat16 [81920, 1536], P(('fsdp', 'dp'))
- input_grad: bfloat16 [131072, 3072], P(('fsdp', 'dp'))
- kernel_grad: float32 [5, 1536], replicated
- norm_grad: float32 [2, 1536], replicated
Inputs may be any that keep to these rules, and one draw needn't show every extreme that they name: `frame_counts`: A device's counts are the lengths of its 8 utterances. A device's total lies from 64 to 256, both reached at every dp index, and the totals of the devices with one dp index sum to 160 times the fsdp axis size. The longest utterance is reached at every dp index. `send_rows`: entry q of a device's list names the local slot whose activation goes to fsdp index q // 2 with the same dp index, as that owner's position q % 2 from this device; the value 256 marks an unused entry. Each live slot is named once, positions for one owner are used from the lowest up, and some device of every dp index fills all 2 positions for every owner. `owner_rows`: entry b names received position p: position p % 2 from fsdp index p // 2 of the same dp index. The 160 entries are distinct and are exactly the positions that senders use for this owner.
All inputs are finite; a program needn't handle non-finite values.
Results may differ from a plain program's by a relative error of at most 0.0085.
Values may be sent and summed in bfloat16 or wider, within the bound.
No kernel may reach another device: no remote copies, remote signals or barrier semaphores. Data moves between devices by JAX's collectives and lax.ppermute only.
A program may use at most 64 MiB of HBM per device.

v0:
```python
import math
import jax
import jax.numpy as jnp
from jax import lax
from jax.sharding import PartitionSpec as P

eps = 1e-05


def conv_module(glu_rows, counts, kernel, gain_vec, bias_vec):
    row_count = glu_rows.shape[0]
    chan_count = kernel.shape[1]
    half_width = kernel.shape[0] // 2
    values = glu_rows.astype(jnp.float32)
    mixed_vals = values[:, :chan_count] * jax.nn.sigmoid(values[:, chan_count:])
    utter_ends = jnp.cumsum(counts)
    position = jnp.arange(row_count, dtype=jnp.int32)
    segment = jnp.sum((position[:, None] >= utter_ends[None, :]).astype(jnp.int32), axis=1)
    is_live = position < utter_ends[-1]
    mixed_vals = jnp.where(is_live[:, None], mixed_vals, 0.0)
    padded = jnp.pad(mixed_vals, ((half_width, half_width), (0, 0)))
    labels = jnp.pad(segment, (half_width, half_width), constant_values=-1)
    conv_out = jnp.zeros((row_count, chan_count), jnp.float32)
    for offset in range(2 * half_width + 1):
        same_utt = labels[offset : offset + row_count] == segment
        conv_out = (
            conv_out
            + jnp.where(same_utt[:, None], padded[offset : offset + row_count], 0.0)
            * kernel[offset]
        )
    center = jnp.mean(conv_out, axis=1, keepdims=True)
    spread = jnp.mean(jnp.square(conv_out - center), axis=1, keepdims=True)
    normed = (conv_out - center) * lax.rsqrt(spread + eps) * gain_vec + bias_vec
    activated = normed * jax.nn.sigmoid(normed)
    return jnp.where(is_live[:, None], activated, 0.0)


def per_device(
    glu_input,
    frame_counts,
    send_rows,
    owner_rows,
    depth_kernel,
    norm_gain,
    norm_bias,
    point_weight,
    cotangent,
):
    counts = frame_counts[0]
    send_slot = send_rows[0]
    owner_slot = owner_rows[0]
    row_count = glu_input.shape[0]
    out_count = point_weight.shape[1]

    def local_pass(glu_rows, kernel, gain_vec, bias_vec):
        return conv_module(glu_rows, counts, kernel, gain_vec, bias_vec)

    activated, pullback = jax.vjp(local_pass, glu_input, depth_kernel, norm_gain, norm_bias)
    activations = activated.astype(jnp.bfloat16)
    produced = jnp.dot(
        activations,
        lax.all_gather(point_weight, "fsdp", axis=0, tiled=True),
        preferred_element_type=jnp.float32,
    ).astype(jnp.bfloat16)
    outgoing = jnp.concatenate([produced, jnp.zeros((1, out_count), jnp.bfloat16)], axis=0)[
        send_slot
    ]
    arrived = lax.all_to_all(outgoing, "fsdp", split_axis=0, concat_axis=0, tiled=True)
    output = arrived[owner_slot]
    parked = jnp.zeros((row_count, out_count), jnp.bfloat16).at[owner_slot].set(cotangent)
    returned = lax.all_to_all(parked, "fsdp", split_axis=0, concat_axis=0, tiled=True)
    home_rows = (
        jnp.zeros((row_count + 1, out_count), jnp.bfloat16).at[send_slot].set(returned)[:row_count]
    )
    grad_acts = lax.dot_general(
        home_rows,
        lax.all_gather(point_weight, "fsdp", axis=0, tiled=True),
        (((1,), (1,)), ((), ())),
        preferred_element_type=jnp.float32,
    ).astype(jnp.bfloat16)
    input_grad, kernel_part, gain_part, bias_part = pullback(grad_acts.astype(jnp.float32))
    totals = lax.psum((kernel_part, jnp.stack([gain_part, bias_part])), ("fsdp", "dp"))
    frame_total = owner_slot.shape[0] * lax.axis_size("fsdp") * lax.axis_size("dp")
    grad_scale = 1.0 / math.sqrt(frame_total)
    return (output, input_grad, totals[0] * grad_scale, totals[1] * grad_scale)


def solution(mesh):
    in_specs = (
        P(("fsdp", "dp"), None),
        P(("fsdp", "dp"), None),
        P(("fsdp", "dp"), None),
        P(("fsdp", "dp"), None),
        P(),
        P(),
        P(),
        P("fsdp", None),
        P(("fsdp", "dp"), None),
    )
    out_specs = (P(("fsdp", "dp"), None), P(("fsdp", "dp"), None), P(), P())
    return jax.shard_map(
        per_device, mesh=mesh, in_specs=in_specs, out_specs=out_specs, check_vma=False
    )
```

profile of v0, /device:TPU:1, one launch (start us, length us, event | category | flops | bytes accessed | tf_op | source)
XLA Modules:
  0.0 759.5 jit_solution(14914906572277938264)
XLA Ops:
  7.2 0.7 all-gather.3.cloned.1.call-update
  7.9 0.7 compare_select_fusion
  8.6 2.1 scatter_custom_fusion
  10.7 1.2 all_to_all.19
  11.9 19.4 %all-to-all-start.1 = ((bf16[128,2,1536]{2,1,0:T(2,128)(2,1)}), bf16[128,2,1536]{2,1,0:T(2,128)(2,1)S(1)}, u32[]{:S(2)}, u32[]{:S(2)}) async-start(bf16[128,2,1536]{2,1,0:T(2,128)(2,1)} %all_to_all.19), calls=%async_computation.1 | async-start | bytes 1572864 | tf_op jit(solution)/shard_map/all_to_all | solution.py:71
  31.5 0.6 slice.55
  32.4 0.7 iota_compare_fusion.1
  33.1 0.3 convert_element_type.24
  33.4 0.4 multiply_select_fusion.4
  33.9 1.3 copy-done
  35.2 1.7 fusion.30
  37.2 21.3 %all-to-all-done.1 = bf16[128,2,1536]{2,1,0:T(2,128)(2,1)S(1)} async-done(((bf16[128,2,1536]{2,1,0:T(2,128)(2,1)}), bf16[128,2,1536]{2,1,0:T(2,128)(2,1)S(1)}, u32[]{:S(2)}, u32[]{:S(2)}) %all-to-all-start.1) | async-done | bytes 786464 | tf_op jit(solution)/shard_map/all_to_all | solution.py:71
  58.8 2.7 scatter_custom_fusion.1
  61.5 458.1 %all-gather.3.cloned.1.call-done = bf16[128,12,1536]{2,1,0:T(8,128)(2,1)} async-done(((bf16[1,12,1536]{2,1,0:T(8,128)(2,1)}), bf16[128,12,1536]{2,1,0:T(8,128)(2,1)}) %all-gather.3.cloned.1.call-update) | async-done | bytes 4718608 | tf_op jit(solution)/shard_map/all_gather | solution.py:62
  519.6 8.2 %reshape.190 = bf16[1536,1536]{1,0:T(8,128)(2,1)} reshape(bf16[128,12,1536]{2,1,0:T(8,128)(2,1)} %all-gather.3.cloned.1.call-done) | data formatting | bytes 9437184
  527.9 3.9 convolution_convert_fusion.1
  531.8 1.3 gather_fusion
  533.1 1.2 all_to_all.16
  534.3 7.4 all-to-all-start
  541.8 4.6 multiply_reduce_fusion
  546.7 1.1 copy-done.3
  547.8 2.4 multiply_reduce_fusion.5
  550.2 0.8 multiply_select_fusion.3
  550.9 1.1 copy-done.1
  552.1 1.4 fusion.4
  553.5 0.4 fusion.28
  554.0 192.0 %all-reduce.15 = (f32[5,1536]{1,0:T(8,128)S(1)}, f32[2,1536]{1,0:T(2,128)S(1)}) all-reduce(f32[5,1536]{1,0:T(8,128)S(1)} %pad_add_fusion.4, f32[2,1536]{1,0:T(2,128)S(1)} %pad_maximum_fusion), channel_id=1, replica_groups=mesh['fsdp'=128,'dp'=4] {'fsdp','dp'}, use_global_device_ids=true, to_apply=%region_14.15 | all-reduce | flops 10752 | bytes 86016 | tf_op jit(solution)/shard_map/psum | solution.py:82
  746.1 1.3 add_convert_fusion
  747.4 0.6 broadcast_multiply_fusion.2
  748.0 0.6 broadcast_multiply_fusion.1
  748.6 2.3 all_to_all.18
  750.9 1.8 gather_fusion.1
  (45 shorter events, 1.6 us)
Async XLA Ops:
  7.2 512.5 %all-gather.3.cloned.1.call-start = ((), (), s32[]{:S(2)}) async-start(), calls=%async_computation.2 | async-start | bytes 6340608 | tf_op jit(solution)/shard_map/all_gather | solution.py:62
  10.7 20.6 %copy-start.10 = (s32[1,8]{1,0:T(1,128)S(1)}, s32[1,8]{1,0:T(1,128)}, u32[]{:S(2)}) copy-start(s32[1,8]{1,0:T(1,128)} %param.10) | copy-start | bytes 100
  10.7 21.4 %copy-start.8 = (s32[1,256]{1,0:T(1,128)S(1)}, s32[1,256]{1,0:T(1,128)}, u32[]{:S(2)}) copy-start(s32[1,256]{1,0:T(1,128)} %param.11) | copy-start | bytes 3076
  10.7 21.5 %copy-start.6 = (f32[5,1536]{1,0:T(8,128)S(1)}, f32[5,1536]{1,0:T(8,128)}, u32[]{:S(2)}) copy-start(f32[5,1536]{1,0:T(8,128)} %param.13) | copy-start | bytes 92164
  11.9 21.1 %copy-start.4 = (bf16[256,3072]{1,0:T(8,128)(2,1)S(1)}, bf16[256,3072]{1,0:T(8,128)(2,1)}, u32[]{:S(2)}) copy-start(bf16[256,3072]{1,0:T(8,128)(2,1)} %param.9) | copy-start | bytes 4718596
  11.9 46.6 %all-to-all-start.1 = ((bf16[128,2,1536]{2,1,0:T(2,128)(2,1)}), bf16[128,2,1536]{2,1,0:T(2,128)(2,1)S(1)}, u32[]{:S(2)}, u32[]{:S(2)}) async-start(bf16[128,2,1536]{2,1,0:T(2,128)(2,1)} %all_to_all.19), calls=%async_computation.1 | async-start | bytes 1572864 | tf_op jit(solution)/shard_map/all_to_all | solution.py:71
  33.4 1.8 copy-start
  35.2 1.7 copy-start.2
  61.5 466.4 %copy-start.7 = (f32[1536]{0:T(1024)S(1)}, f32[1536]{0:T(1024)}, u32[]{:S(2)}) copy-start(f32[1536]{0:T(1024)} %param.14) | copy-start | bytes 18436
  61.5 466.4 %copy-start.9 = (f32[1536]{0:T(1024)S(1)}, f32[1536]{0:T(1024)}, u32[]{:S(2)}) copy-start(f32[1536]{0:T(1024)} %param.15) | copy-start | bytes 18436
  533.1 8.6 %copy-start.5 = (bf16[257,1536]{1,0:T(8,128)(2,1)S(1)}, bf16[257,1536]{1,0:T(8,128)(2,1)}, u32[]{:S(2)}) copy-start(bf16[257,1536]{1,0:T(8,128)(2,1)} %scatter_custom_fusion.1) | copy-start | bytes 2368516
  534.3 214.3 %all-to-all-start = ((bf16[128,2,1536]{2,1,0:T(2,128)(2,1)}), bf16[128,2,1536]{2,1,0:T(2,128)(2,1)}, u32[]{:S(2)}, u32[]{:S(2)}) async-start(bf16[128,2,1536]{2,1,0:T(2,128)(2,1)} %all_to_all.16), calls=%async_computation | async-start | bytes 1572864 | tf_op jit(solution)/shard_map/all_to_all | solution.py:68
  546.4 1.4 copy-start.3
  550.2 1.9 copy-start.1
Sparse Core Ops, SparseCore 0:
  10.1 509.5 all-gather.2
where the time goes:
time: 760 us
  waiting for transfers between devices  480 us (63%)
  blocking collectives  192 us (25%)
  starting transfers between devices  26.9 us (4%)
  local copies, waits for them, and re-layouts  25.3 us (3%)
  between operations  14.4 us (2%)
  other arithmetic  12.3 us (2%)
  matrix products  8.52 us (1%)
    all_gather x1, waiting for transfers between devices, per_device(): lax.all_gather(point_weight, 'fsdp', axis=0, tiled=True)  458 us
    psum x1, blocking collectives, per_device(): lax.psum((kernel_part, jnp.stack([gain_part, bias_part])), ('fsdp', 'dp'))  192 us
    all_to_all x1, waiting for transfers between devices, per_device(): lax.all_to_all(parked, 'fsdp', split_axis=0, concat_axis=0, tiled=True)  21.3 us
    all_to_all x1, starting transfers between devices, per_device(): lax.all_to_all(parked, 'fsdp', split_axis=0, concat_axis=0, tiled=True)  19.4 us
  transfers between devices with their start and end apart: 3, of which 2 were waited for; matrix products, arithmetic and copies ran while one was open for 3% of the time, Pallas kernels for 0%

commit v1 on v0

--- a/solution.py
+++ b/solution.py
@@ -59,7 +59,9 @@
     activations = activated.astype(jnp.bfloat16)
     produced = jnp.dot(
         activations,
-        lax.all_gather(point_weight, "fsdp", axis=0, tiled=True),
+        jnp.concatenate(
+            lax.all_to_all(jnp.stack([point_weight] * lax.axis_size("fsdp")), "fsdp", 0, 0), axis=0
+        ),
         preferred_element_type=jnp.float32,
     ).astype(jnp.bfloat16)
     outgoing = jnp.concatenate([produced, jnp.zeros((1, out_count), jnp.bfloat16)], axis=0)[

time: 760 us -> 836 us (1.10)
  blocking collectives: 192 us -> 230 us
  waiting for transfers between devices: 480 us -> 500 us
  local copies, waits for them, and re-layouts: 25.3 us -> 35.7 us
    all_to_all x1, waiting for transfers between devices: 21.3 us -> 143 us  [per_device(): lax.all_to_all(jnp.stack([point_weight] * lax.axis_size('fsdp')), 'fsdp',...]
    all_gather x1, waiting for transfers between devices: 458 us -> 356 us  [per_device(): lax.all_gather(point_weight, 'fsdp', axis=0, tiled=True)]
    all_to_all x0 -> x1, blocking collectives: none -> 42.7 us  [per_device(): lax.all_to_all(parked, 'fsdp', split_axis=0, concat_axis=0, tiled=True)]
    all_to_all x1, starting transfers between devices: 7.43 us -> 24.2 us  [per_device(): lax.all_to_all(outgoing, 'fsdp', split_axis=0, concat_axis=0, tiled=True)]
    all_to_all x1, starting transfers between devices: 19.4 us -> 8.26 us  [per_device(): lax.all_to_all(jnp.stack([point_weight] * lax.axis_size('fsdp')), 'fsdp',...]
  transfers between devices with their start and end apart: 3 -> 3, of which waited for: 2 -> 2; matrix products, arithmetic and copies ran while one was open for 3% -> 5% of each run, Pallas kernels for 0% -> 0%
where the time goes in v1:
time: 836 us; the launch traced here: 835 us
  waiting for transfers between devices  500 us (60%)
  blocking collectives  230 us (28%)
  local copies, waits for them, and re-layouts  35.7 us (4%)
  starting transfers between devices  32.5 us (4%)
  between operations  14.4 us (2%)
  other arithmetic  13.8 us (2%)
  matrix products  8.49 us (1%)
    all_gather x1, waiting for transfers between devices, per_device(): lax.all_gather(point_weight, 'fsdp', axis=0, tiled=True)  356 us
    psum x1, blocking collectives, per_device(): lax.psum((kernel_part, jnp.stack([gain_part, bias_part])), ('fsdp', 'dp'))  187 us
    all_to_all x1, waiting for transfers between devices, per_device(): lax.all_to_all(jnp.stack([point_weight] * lax.axis_size('fsdp')), 'fsdp',...  143 us
    all_to_all x1, blocking collectives, per_device(): lax.all_to_all(parked, 'fsdp', split_axis=0, concat_axis=0, tiled=True)  42.7 us
    all_to_all x1, starting transfers between devices, per_device(): lax.all_to_all(outgoing, 'fsdp', split_axis=0, concat_axis=0, tiled=True)  24.2 us
  transfers between devices with their start and end apart: 3, of which 2 were waited for; matrix products, arithmetic and copies ran while one was open for 5% of the time, Pallas kernels for 0%

profile of v1, /device:TPU:1, one launch (start us, length us, event | category | flops | bytes accessed | tf_op | source)
XLA Modules:
  0.0 835.0 jit_solution(2222280546742852493)
XLA Ops:
  7.2 0.7 compare_select_fusion
  7.8 2.1 scatter_custom_fusion
  10.3 42.7 %all_to_all.29 = bf16[128,2,1536]{2,1,0:T(2,128)(2,1)} all-to-all(bf16[128,2,1536]{2,1,0:T(2,128)(2,1)S(1)} %all_to_all.23), channel_id=1, replica_groups=mesh['fsdp'=128,'dp'=4] {'fsdp'}, dimensions={0} | all-to-all | bytes 1572864 | tf_op jit(solution)/shard_map/all_to_all | solution.py:73
  53.0 3.4 stack.4
  56.4 8.3 all-to-all-start
  64.7 0.7 all-gather.3.cloned.1.call-update
  65.4 1.8 convert_element_type.24
  67.4 0.8 slice.55
  68.2 0.7 iota_compare_fusion.1
  69.6 1.7 fusion.30
  71.7 0.8 copy-done.4
  72.8 2.7 scatter_custom_fusion.1
  75.5 143.3 %all-to-all-done = bf16[128,12,1536]{2,1,0:T(8,128)(2,1)} async-done(((bf16[128,12,1536]{2,1,0:T(8,128)(2,1)}), bf16[128,12,1536]{2,1,0:T(8,128)(2,1)}, u32[]{:S(2)}, u32[]{:S(2)}) %all-to-all-start) | async-done | bytes 4718624 | tf_op jit(solution)/shard_map/all_to_all | solution.py:63
  218.8 8.2 reshape.155
  227.0 3.9 convolution_convert_fusion.1
  230.9 1.3 gather_fusion
  232.2 1.2 all_to_all.20
  233.4 24.2 %all-to-all-start.1 = ((bf16[128,2,1536]{2,1,0:T(2,128)(2,1)}), bf16[128,2,1536]{2,1,0:T(2,128)(2,1)}, u32[]{:S(2)}, u32[]{:S(2)}) async-start(bf16[128,2,1536]{2,1,0:T(2,128)(2,1)} %all_to_all.20), calls=%async_computation.1 | async-start | bytes 1572864 | tf_op jit(solution)/shard_map/all_to_all | solution.py:70
  257.7 356.2 %all-gather.3.cloned.1.call-done = bf16[128,12,1536]{2,1,0:T(8,128)(2,1)} async-done(((bf16[1,12,1536]{2,1,0:T(8,128)(2,1)}), bf16[128,12,1536]{2,1,0:T(8,128)(2,1)}) %all-gather.3.cloned.1.call-update) | async-done | bytes 4718608 | tf_op jit(solution)/shard_map/all_gather | solution.py:79
  613.8 8.2 reshape.196
  622.1 4.6 multiply_reduce_fusion
  627.0 1.1 copy-done.3
  628.1 2.4 multiply_reduce_fusion.5
  630.5 0.8 multiply_select_fusion.3
  631.2 1.1 copy-done.1
  632.3 1.4 fusion.4
  634.3 187.3 %all-reduce.15 = (f32[5,1536]{1,0:T(8,128)S(1)}, f32[2,1536]{1,0:T(2,128)S(1)}) all-reduce(f32[5,1536]{1,0:T(8,128)S(1)} %pad_add_fusion.4, f32[2,1536]{1,0:T(2,128)S(1)} %pad_maximum_fusion), channel_id=1, replica_groups=mesh['fsdp'=128,'dp'=4] {'fsdp','dp'}, use_global_device_ids=true, to_apply=%region_14.15 | all-reduce | flops 10752 | bytes 86016 | tf_op jit(solution)/shard_map/psum | solution.py:84
  821.6 1.3 add_convert_fusion
  822.9 0.6 broadcast_multiply_fusion.2
  823.5 0.6 broadcast_multiply_fusion.1
  824.1 2.3 all_to_all.22
  826.4 1.8 gather_fusion.1
  (50 shorter events, 2.8 us)
Async XLA Ops:
  9.9 43.0 %copy-start.6 = (bf16[12,1536]{1,0:T(8,128)(2,1)S(1)}, bf16[12,1536]{1,0:T(8,128)(2,1)}, u32[]{:S(2)}) copy-start(bf16[12,1536]{1,0:T(8,128)(2,1)} %param.16) | copy-start | bytes 110596
  56.4 162.5 %all-to-all-start = ((bf16[128,12,1536]{2,1,0:T(8,128)(2,1)}), bf16[128,12,1536]{2,1,0:T(8,128)(2,1)}, u32[]{:S(2)}, u32[]{:S(2)}) async-start(bf16[128,12,1536]{2,1,0:T(8,128)(2,1)} %stack.4), calls=%async_computation | async-start | bytes 12582912 | tf_op jit(solution)/shard_map/all_to_all | solution.py:63
  64.6 549.2 %all-gather.3.cloned.1.call-start = ((), (), s32[]{:S(2)}) async-start(), calls=%async_computation.3 | async-start | bytes 6340608 | tf_op jit(solution)/shard_map/all_gather | solution.py:79
  65.4 1.8 copy-start.11
  65.4 3.5 copy-start.9
  65.4 3.6 copy-start.7
  67.2 2.4 copy-start
  69.6 1.7 copy-start.2
  71.3 1.1 copy-start.4
  75.5 151.5 %copy-start.8 = (f32[1536]{0:T(1024)S(1)}, f32[1536]{0:T(1024)}, u32[]{:S(2)}) copy-start(f32[1536]{0:T(1024)} %param.14) | copy-start | bytes 18436
  75.5 151.5 %copy-start.10 = (f32[1536]{0:T(1024)S(1)}, f32[1536]{0:T(1024)}, u32[]{:S(2)}) copy-start(f32[1536]{0:T(1024)} %param.15) | copy-start | bytes 18436
  233.4 590.8 %all-to-all-start.1 = ((bf16[128,2,1536]{2,1,0:T(2,128)(2,1)}), bf16[128,2,1536]{2,1,0:T(2,128)(2,1)}, u32[]{:S(2)}, u32[]{:S(2)}) async-start(bf16[128,2,1536]{2,1,0:T(2,128)(2,1)} %all_to_all.20), calls=%async_computation.1 | async-start | bytes 1572864 | tf_op jit(solution)/shard_map/all_to_all | solution.py:70
  257.6 364.4 %copy-start.5 = (bf16[257,1536]{1,0:T(8,128)(2,1)S(1)}, bf16[257,1536]{1,0:T(8,128)(2,1)}, u32[]{:S(2)}) copy-start(bf16[257,1536]{1,0:T(8,128)(2,1)} %scatter_custom_fusion.1) | copy-start | bytes 2368516
  626.7 1.4 copy-start.3
  630.5 1.9 copy-start.1
Sparse Core Ops, SparseCore 0:
  67.5 546.2 all-gather.2
